TPU v7x, 512 devices: a whole 4x8x8 slice. The times are simulated.
512 devices in a mesh: seq: 64 (over z_hi, y, core), ch: 8 (over x, z_lo).
Axes of the slice: x: 4, y: 8, z: 8 (z_hi: 4, z_lo: 2; z = z_hi * 2 + z_lo), core: 2. Of those that a mesh axis runs over, the one named last changes fastest.
Arguments:
- inputs: bfloat16 [262144, 2048], P('seq', 'ch'), may hold values from -6 to 6
- first_factor: bfloat16 [512, 512], P('ch'), may hold values from -0.25 to 0.25
- twiddle: float32 [512, 512], P('seq'), may hold values from -4 to 4
- second_factor: bfloat16 [512, 512], P('ch'), may hold values from -0.25 to 0.25
- block_first: bfloat16 [64, 32, 32], P('ch'), may hold values from -1 to 1
- block_second: bfloat16 [32, 64, 64], P('ch'), may hold values from -0.75 to 0.75
Outputs:
- mixed_out: bfloat16 [262144, 2048], P('seq', 'ch')
All inputs are finite; a program needn't handle non-finite values.
Results may differ from a plain program's by a relative error of at most 0.007.
Values may be sent and summed in bfloat16 or wider, within the bound.
No kernel may reach another device: no remote copies, remote signals or barrier semaphores. Data moves between devices by JAX's collectives and lax.ppermute only.
A program may use at most 128 MiB of HBM per device.

v0:
```python
import jax
import jax.numpy as jnp
from jax import lax
from jax.sharding import PartitionSpec as P

BLOCK = 512
CHUNKS = 1


def channel_weights(block_first, block_second, n_ch):
    n_a, n_m, n_b = block_first.shape
    m_l = n_m // n_ch
    bf = jnp.transpose(block_first, (1, 0, 2))
    bf = bf.reshape(n_ch, m_l, n_a, 1, n_b)
    eye_a = jnp.eye(n_a, dtype=jnp.bool_).reshape(1, 1, n_a, n_a, 1)
    w1t = jnp.where(eye_a, bf, jnp.zeros((), bf.dtype))
    w1t = w1t.reshape(n_ch * m_l * n_a, n_a * n_b)
    n_m2, n_p, n_a2 = block_second.shape
    a_l = n_a2 // n_ch
    bs = block_second.reshape(n_m2, n_p, n_ch, a_l)
    bs = jnp.transpose(bs, (2, 0, 3, 1))
    bs = bs.reshape(n_ch, n_m2, a_l, 1, n_p)
    eye_m = jnp.eye(n_m2, dtype=jnp.bool_).reshape(1, n_m2, 1, n_m2, 1)
    w2 = jnp.where(eye_m, bs, jnp.zeros((), bs.dtype))
    w2 = w2.reshape(n_ch * n_m2 * a_l, n_m2 * n_p)
    return (w1t, w2)


def make_local(n_seq, n_ch):

    def local(inputs, first_factor, twiddle, second_factor, block_first, block_second):
        tok_rows, channels = inputs.shape
        outer_rows = tok_rows // BLOCK
        token_grid = inputs.reshape(outer_rows, BLOCK, channels)
        rows = first_factor.shape[0]
        pair = jnp.concatenate([first_factor, second_factor], axis=0)
        spread = jnp.broadcast_to(pair[None], (n_ch,) + pair.shape)
        both = lax.all_to_all(spread, "ch", split_axis=0, concat_axis=0, tiled=True)
        both = both.reshape(n_ch, 2, rows, BLOCK)
        full_first = both[:, 0].reshape(BLOCK, BLOCK)
        full_second = both[:, 1].reshape(BLOCK, BLOCK)
        twiddle_t = jnp.transpose(twiddle)
        token_f32 = lax.optimization_barrier(token_grid)
        w1t, w2 = channel_weights(block_first, block_second, n_ch)
        contract = (((1,), (1,)), ((), ()))
        width = BLOCK // CHUNKS
        outs = []
        for q in range(CHUNKS):
            lo = q * width
            first = lax.dot_general(
                full_first[lo : lo + width],
                token_grid,
                contract,
                preferred_element_type=jnp.float32,
            )
            twisted = (first * twiddle_t[lo : lo + width, :, None]).astype(jnp.bfloat16)
            twisted, w1t, w2 = lax.optimization_barrier((twisted, w1t, w2))
            gathered = lax.all_to_all(twisted, "seq", split_axis=0, concat_axis=1, tiled=True)
            mixed = lax.dot_general(
                full_second, gathered, contract, preferred_element_type=jnp.float32
            ).astype(jnp.bfloat16)
            returned = lax.all_to_all(mixed, "seq", split_axis=0, concat_axis=1, tiled=True)
            gated = (
                token_f32[:, lo : lo + width].astype(jnp.float32) * returned.astype(jnp.float32)
            ).astype(jnp.bfloat16)
            gated = gated.reshape(outer_rows * width, channels)
            middle_t = lax.dot_general(
                w1t, gated, contract, preferred_element_type=jnp.float32
            ).astype(jnp.bfloat16)
            middle_t = middle_t.reshape(n_ch, channels // n_ch, outer_rows * width)
            recv = lax.all_to_all(middle_t, "ch", split_axis=0, concat_axis=0, tiled=True)
            recv = recv.reshape(channels, outer_rows * width)
            result = lax.dot_general(
                recv, w2, (((0,), (0,)), ((), ())), preferred_element_type=jnp.float32
            ).astype(jnp.bfloat16)
            outs.append(result.reshape(outer_rows, width, channels))
        out = jnp.concatenate(outs, axis=1)
        return out.reshape(tok_rows, channels)

    return local


def solution(mesh):
    placed = (
        P("seq", "ch"),
        P("ch", None),
        P("seq", None),
        P("ch", None),
        P("ch", None, None),
        P("ch", None, None),
    )
    return jax.shard_map(
        make_local(mesh.shape["seq"], mesh.shape["ch"]),
        mesh=mesh,
        in_specs=placed,
        out_specs=P("seq", "ch"),
        check_vma=False,
    )
```

profile of v0, /device:TPU:41, one launch (start us, length us, event | category | flops | bytes accessed | tf_op | source)
XLA Modules:
  0.0 202.5 jit_solution(12817067652406120706)
XLA Ops:
  0.0 0.0 copy-start.1
  0.0 0.0 copy-start.2
  0.0 0.9 pad_maximum_fusion
  0.9 1.1 broadcast_in_dim.49
  2.0 5.8 %all-to-all-start = ((bf16[8,128,512]{2,1,0:T(8,128)(2,1)}), bf16[8,128,512]{2,1,0:T(8,128)(2,1)S(1)}, u32[]{:S(2)}, u32[]{:S(2)}) async-start(bf16[8,128,512]{2,1,0:T(8,128)(2,1)} %broadcast_in_dim.49), calls=%async_computation | async-start | bytes 2097152 | tf_op jit(solution)/shard_map/all_to_all | solution.py:38
  7.8 0.0 copy-done.1
  7.8 0.6 copy.16
  8.5 0.0 copy-done.2
  8.5 0.0 copy-start
  8.5 0.0 copy-start.3
  8.5 0.1 copy.17
  8.6 0.2 broadcast_select_fusion.1
  8.8 0.2 select_n.19
  9.0 1.8 broadcast_select_fusion
  10.9 1.4 select_n.17
  12.3 10.1 %all-to-all-done = bf16[8,128,512]{2,1,0:T(8,128)(2,1)S(1)} async-done(((bf16[8,128,512]{2,1,0:T(8,128)(2,1)}), bf16[8,128,512]{2,1,0:T(8,128)(2,1)S(1)}, u32[]{:S(2)}, u32[]{:S(2)}) %all-to-all-start) | async-done | bytes 1048608 | tf_op jit(solution)/shard_map/all_to_all | solution.py:38
  22.4 0.1 fusion.7
  22.5 0.0 copy-done
  22.5 0.0 copy-done.3
  22.5 1.5 multiply_convert_fusion
  24.0 1.2 copy.19
  25.2 74.3 %all_to_all.37 = bf16[512,8,256]{2,1,0:T(8,128)(2,1)S(1)} all-to-all(bf16[512,8,256]{2,1,0:T(8,128)(2,1)S(1)} %copy.19), channel_id=1, replica_groups=mesh['seq'=64,'ch'=8] {'seq'}, dimensions={0} | all-to-all | bytes 4194304 | tf_op jit(solution)/shard_map/all_to_all | solution.py:58
  99.5 1.3 fusion.4
  100.7 2.5 %copy.21 = bf16[512,8,256]{2,1,0:T(8,128)(2,1)} copy(bf16[512,8,256]{2,0,1:T(8,128)(2,1)S(1)} %fusion.4) | data formatting | bytes 4194304 | tf_op jit(solution)/shard_map/convert_element_type | solution.py:61
  103.2 8.7 %all-to-all-start.2 = ((bf16[512,8,256]{2,1,0:T(8,128)(2,1)}), bf16[512,8,256]{2,1,0:T(8,128)(2,1)S(1)}, u32[]{:S(2)}, u32[]{:S(2)}) async-start(bf16[512,8,256]{2,1,0:T(8,128)(2,1)} %copy.21), calls=%async_computation.2 | async-start | bytes 4194304 | tf_op jit(solution)/shard_map/all_to_all | solution.py:62
  111.9 52.2 %all-to-all-done.2 = bf16[512,8,256]{2,1,0:T(8,128)(2,1)S(1)} async-done(((bf16[512,8,256]{2,1,0:T(8,128)(2,1)}), bf16[512,8,256]{2,1,0:T(8,128)(2,1)S(1)}, u32[]{:S(2)}, u32[]{:S(2)}) %all-to-all-start.2) | async-done | bytes 2097184 | tf_op jit(solution)/shard_map/all_to_all | solution.py:62
  164.1 2.1 %fusion = bf16[8,512,256]{2,1,0:T(8,128)(2,1)S(1)} fusion(bf16[8,512,256]{2,1,0:T(8,128)(2,1)} %bitcast.52, bf16[64,8,8,256]{3,2,1,0:T(8,128)(2,1)S(1)} %bitcast.48), kind=kLoop, calls=%fused_computation.4 | loop fusion | flops 4194304 | bytes 6291456 | tf_op jit(solution)/shard_map/convert_element_type | solution.py:65
  166.2 0.7 convolution_convert_fusion.1
  166.9 33.5 %all_to_all.38 = bf16[8,32,4096]{2,1,0:T(8,128)(2,1)S(1)} all-to-all(bf16[8,32,4096]{2,1,0:T(8,128)(2,1)S(1)} %bitcast.50), channel_id=1, replica_groups=mesh['seq'=64,'ch'=8] {'ch'}, dimensions={0} | all-to-all | bytes 4194304 | tf_op jit(solution)/shard_map/all_to_all | solution.py:71
  200.5 2.1 %convolution_convert_fusion = bf16[4096,256]{1,0:T(8,128)(2,1)} fusion(bf16[256,4096]{1,0:T(8,128)(2,1)S(1)} %bitcast.47, bf16[256,256]{1,0:T(8,128)(2,1)S(1)} %select_n.19), kind=kOutput, calls=%fused_computation | convolution fusion | flops 537919488 | bytes 4325376 | tf_op jit(solution)/shard_map/dot_general | solution.py:73
  (2 shorter events, 0.0 us)
Async XLA Ops:
  0.0 7.8 %copy-start.1 = (bf16[8,32,32]{2,1,0:T(8,128)(2,1)S(1)}, bf16[8,32,32]{2,1,0:T(8,128)(2,1)}, u32[]{:S(2)}) copy-start(bf16[8,32,32]{2,1,0:T(8,128)(2,1)} %param.10) | copy-start | bytes 49156
  0.0 8.5 %copy-start.2 = (bf16[4,64,64]{2,1,0:T(8,128)(2,1)S(1)}, bf16[4,64,64]{2,1,0:T(8,128)(2,1)}, u32[]{:S(2)}) copy-start(bf16[4,64,64]{2,1,0:T(8,128)(2,1)} %param.11) | copy-start | bytes 98308
  2.0 20.4 %all-to-all-start = ((bf16[8,128,512]{2,1,0:T(8,128)(2,1)}), bf16[8,128,512]{2,1,0:T(8,128)(2,1)S(1)}, u32[]{:S(2)}, u32[]{:S(2)}) async-start(bf16[8,128,512]{2,1,0:T(8,128)(2,1)} %broadcast_in_dim.49), calls=%async_computation | async-start | bytes 2097152 | tf_op jit(solution)/shard_map/all_to_all | solution.py:38
  8.5 14.0 %copy-start = (bf16[4096,256]{1,0:T(8,128)(2,1)S(1)}, bf16[4096,256]{1,0:T(8,128)(2,1)}, u32[]{:S(2)}) copy-start(bf16[4096,256]{1,0:T(8,128)(2,1)} %param.6) | copy-start | bytes 6291460
  8.5 14.0 %copy-start.3 = (f32[8,512]{1,0:T(8,128)S(1)}, f32[8,512]{1,0:T(8,128)}, u32[]{:S(2)}) copy-start(f32[8,512]{1,0:T(8,128)} %param.8) | copy-start | bytes 49156
  103.2 60.8 %all-to-all-start.2 = ((bf16[512,8,256]{2,1,0:T(8,128)(2,1)}), bf16[512,8,256]{2,1,0:T(8,128)(2,1)S(1)}, u32[]{:S(2)}, u32[]{:S(2)}) async-start(bf16[512,8,256]{2,1,0:T(8,128)(2,1)} %copy.21), calls=%async_computation.2 | async-start | bytes 4194304 | tf_op jit(solution)/shard_map/all_to_all | solution.py:62
where the time goes:
time: 203 us
  blocking collectives  108 us (53%)
  waiting for transfers between devices  62.2 us (31%)
  starting transfers between devices  14.5 us (7%)
  local copies, waits for them, and re-layouts  7.24 us (4%)
  matrix products  5.56 us (3%)
  other arithmetic  5.05 us (2%)
    all_to_all x1, blocking collectives, local(): lax.all_to_all(twisted, 'seq', split_axis=0, concat_axis=1, tiled=True)  74.3 us
    all_to_all x1, waiting for transfers between devices, local(): lax.all_to_all(mixed, 'seq', split_axis=0, concat_axis=1, tiled=True)  52.2 us
    all_to_all x1, blocking collectives, local(): lax.all_to_all(middle_t, 'ch', split_axis=0, concat_axis=0, tiled=True)  33.5 us
    all_to_all x1, waiting for transfers between devices, local(): both = lax.all_to_all(spread, 'ch', split_axis=0, concat_axis=0, tiled=True)  10.1 us
    all_to_all x1, starting transfers between devices, local(): lax.all_to_all(mixed, 'seq', split_axis=0, concat_axis=1, tiled=True)  8.66 us
    all_to_all x1, starting transfers between devices, local(): both = lax.all_to_all(spread, 'ch', split_axis=0, concat_axis=0, tiled=True)  5.83 us
  transfers between devices with their start and end apart: 2, of which 2 were waited for; matrix products, arithmetic and copies ran while one was open for 2% of the time, Pallas kernels for 0%

commit v1 on v0

--- a/solution.py
+++ b/solution.py
@@ -59,7 +59,12 @@
             mixed = lax.dot_general(
                 full_second, gathered, contract, preferred_element_type=jnp.float32
             ).astype(jnp.bfloat16)
-            returned = lax.all_to_all(mixed, "seq", split_axis=0, concat_axis=1, tiled=True)
+            returned = jnp.concatenate(
+                lax.all_to_all(
+                    jnp.stack(jnp.split(mixed, lax.axis_size("seq"), axis=0)), "seq", 0, 0
+                ),
+                axis=1,
+            )
             gated = (
                 token_f32[:, lo : lo + width].astype(jnp.float32) * returned.astype(jnp.float32)
             ).astype(jnp.bfloat16)

time: 203 us -> 241 us (1.19)
  local copies, waits for them, and re-layouts: 7.24 us -> 43.7 us
  waiting for transfers between devices: 62.2 us -> 65.6 us
    unnamed x9 -> x74, local copies, waits for them, and re-layouts: 0.12 us -> 40.1 us
    all_to_all x1, waiting for transfers between devices: 10.1 us -> 13.5 us  [local(): both = lax.all_to_all(spread, 'ch', split_axis=0, concat_axis=0, tiled=True)]
    convert_element_type x1 -> x0, local copies, waits for them, and re-layouts: 2.5 us -> none  [local(): mixed = lax.dot_general(full_second, gathered, contract, preferred_elemen...]
  transfers between devices with their start and end apart: 2 -> 2, of which waited for: 2 -> 2; matrix products, arithmetic and copies ran while one was open for 2% -> 0% of each run, Pallas kernels for 0% -> 0%
where the time goes in v1:
time: 241 us
  blocking collectives  108 us (45%)
  waiting for transfers between devices  65.6 us (27%)
  local copies, waits for them, and re-layouts  43.7 us (18%)
  starting transfers between devices  14.5 us (6%)
  matrix products  5.57 us (2%)
  other arithmetic  3.38 us (1%)
    all_to_all x1, blocking collectives, local(): lax.all_to_all(twisted, 'seq', split_axis=0, concat_axis=1, tiled=True)  74.3 us
    all_to_all x1, waiting for transfers between devices, local(): lax.all_to_all(jnp.stack(jnp.split(mixed, lax.axis_size('seq'), axis=0)),...  52.2 us
    unnamed x74, local copies, waits for them, and re-layouts  40.1 us
    all_to_all x1, blocking collectives, local(): lax.all_to_all(middle_t, 'ch', split_axis=0, concat_axis=0, tiled=True)  33.5 us
    all_to_all x1, waiting for transfers between devices, local(): both = lax.all_to_all(spread, 'ch', split_axis=0, concat_axis=0, tiled=True)  13.5 us
    all_to_all x1, starting transfers between devices, local(): lax.all_to_all(jnp.stack(jnp.split(mixed, lax.axis_size('seq'), axis=0)),...  8.66 us
    all_to_all x1, starting transfers between devices, local(): both = lax.all_to_all(spread, 'ch', split_axis=0, concat_axis=0, tiled=True)  5.83 us
  transfers between devices with their start and end apart: 2, of which 2 were waited for; matrix products, arithmetic and copies ran while one was open for 0% of the time, Pallas kernels for 0%

profile of v1, /device:TPU:41, one launch (start us, length us, event | category | flops | bytes accessed | tf_op | source)
XLA Modules:
  0.0 240.8 jit_solution(4558365037833800233)
XLA Ops:
  0.0 0.9 pad_maximum_fusion
  0.9 1.1 broadcast_in_dim.49
  2.0 5.8 %all-to-all-start = ((bf16[8,128,512]{2,1,0:T(8,128)(2,1)}), bf16[8,128,512]{2,1,0:T(8,128)(2,1)S(1)}, u32[]{:S(2)}, u32[]{:S(2)}) async-start(bf16[8,128,512]{2,1,0:T(8,128)(2,1)} %broadcast_in_dim.49), calls=%async_computation | async-start | bytes 2097152 | tf_op jit(solution)/shard_map/all_to_all | solution.py:38
  8.9 13.5 %all-to-all-done = bf16[8,128,512]{2,1,0:T(8,128)(2,1)S(1)} async-done(((bf16[8,128,512]{2,1,0:T(8,128)(2,1)}), bf16[8,128,512]{2,1,0:T(8,128)(2,1)S(1)}, u32[]{:S(2)}, u32[]{:S(2)}) %all-to-all-start) | async-done | bytes 1048608 | tf_op jit(solution)/shard_map/all_to_all | solution.py:38
  22.5 1.5 multiply_convert_fusion
  24.0 1.2 copy.19
  25.2 74.3 %all_to_all.33 = bf16[512,8,256]{2,1,0:T(8,128)(2,1)S(1)} all-to-all(bf16[512,8,256]{2,1,0:T(8,128)(2,1)S(1)} %copy.19), channel_id=1, replica_groups=mesh['seq'=64,'ch'=8] {'seq'}, dimensions={0} | all-to-all | bytes 4194304 | tf_op jit(solution)/shard_map/all_to_all | solution.py:58
  99.5 1.3 fusion.4
  100.7 0.6 constant_dynamic-update-slice_fusion.63
  102.0 0.6 constant_dynamic-update-slice_fusion.61
  103.8 0.6 constant_dynamic-update-slice_fusion.58
  105.7 0.6 constant_dynamic-update-slice_fusion.55
  107.5 0.6 constant_dynamic-update-slice_fusion.52
  109.4 0.6 constant_dynamic-update-slice_fusion.49
  111.3 0.6 constant_dynamic-update-slice_fusion.46
  111.9 0.6 constant_dynamic-update-slice_fusion.45
  113.7 0.6 constant_dynamic-update-slice_fusion.42
  115.6 0.6 constant_dynamic-update-slice_fusion.39
  117.5 0.6 constant_dynamic-update-slice_fusion.36
  119.3 0.6 constant_dynamic-update-slice_fusion.33
  121.2 0.6 constant_dynamic-update-slice_fusion.30
  123.0 0.6 constant_dynamic-update-slice_fusion.27
  123.7 0.6 constant_dynamic-update-slice_fusion.26
  125.5 0.6 constant_dynamic-update-slice_fusion.23
  127.4 0.6 constant_dynamic-update-slice_fusion.20
  140.4 8.7 %all-to-all-start.2 = ((bf16[64,8,8,256]{3,1,2,0:T(8,128)(2,1)}), bf16[64,8,8,256]{3,1,2,0:T(8,128)(2,1)S(1)}, u32[]{:S(2)}, u32[]{:S(2)}) async-start(bf16[64,8,8,256]{3,1,2,0:T(8,128)(2,1)} %constant_dynamic-update-slice_fusion), calls=%async_computation.2 | async-start | bytes 4194304 | tf_op jit(solution)/shard_map/all_to_all | solution.py:63
  149.0 52.2 %all-to-all-done.2 = bf16[64,8,8,256]{3,1,2,0:T(8,128)(2,1)S(1)} async-done(((bf16[64,8,8,256]{3,1,2,0:T(8,128)(2,1)}), bf16[64,8,8,256]{3,1,2,0:T(8,128)(2,1)S(1)}, u32[]{:S(2)}, u32[]{:S(2)}) %all-to-all-start.2) | async-done | bytes 2097184 | tf_op jit(solution)/shard_map/all_to_all | solution.py:63
  201.8 1.0 copy-done.1
  202.8 1.6 fusion
  204.4 0.7 convolution_convert_fusion.1
  205.2 33.5 %all_to_all.34 = bf16[8,32,4096]{2,1,0:T(8,128)(2,1)S(1)} all-to-all(bf16[8,32,4096]{2,1,0:T(8,128)(2,1)S(1)} %bitcast.299), channel_id=1, replica_groups=mesh['seq'=64,'ch'=8] {'ch'}, dimensions={0} | all-to-all | bytes 4194304 | tf_op jit(solution)/shard_map/all_to_all | solution.py:76
  238.7 2.1 convolution_convert_fusion
  (66 shorter events, 30.8 us)
Async XLA Ops:
  0.0 7.8 %copy-start.2 = (bf16[8,32,32]{2,1,0:T(8,128)(2,1)S(1)}, bf16[8,32,32]{2,1,0:T(8,128)(2,1)}, u32[]{:S(2)}) copy-start(bf16[8,32,32]{2,1,0:T(8,128)(2,1)} %param.10) | copy-start | bytes 49156
  0.0 7.9 %copy-start.3 = (bf16[4,64,64]{2,1,0:T(8,128)(2,1)S(1)}, bf16[4,64,64]{2,1,0:T(8,128)(2,1)}, u32[]{:S(2)}) copy-start(bf16[4,64,64]{2,1,0:T(8,128)(2,1)} %param.11) | copy-start | bytes 98308
  2.0 20.4 %all-to-all-start = ((bf16[8,128,512]{2,1,0:T(8,128)(2,1)}), bf16[8,128,512]{2,1,0:T(8,128)(2,1)S(1)}, u32[]{:S(2)}, u32[]{:S(2)}) async-start(bf16[8,128,512]{2,1,0:T(8,128)(2,1)} %broadcast_in_dim.49), calls=%async_computation | async-start | bytes 2097152 | tf_op jit(solution)/shard_map/all_to_all | solution.py:38
  7.9 14.6 %copy-start.4 = (f32[8,512]{1,0:T(8,128)S(1)}, f32[8,512]{1,0:T(8,128)}, u32[]{:S(2)}) copy-start(f32[8,512]{1,0:T(8,128)} %param.8) | copy-start | bytes 49156
  8.9 13.6 %copy-start = (bf16[4096,256]{1,0:T(8,128)(2,1)S(1)}, bf16[4096,256]{1,0:T(8,128)(2,1)}, u32[]{:S(2)}) copy-start(bf16[4096,256]{1,0:T(8,128)(2,1)} %param.6) | copy-start | bytes 6291460
  140.4 60.9 %all-to-all-start.2 = ((bf16[64,8,8,256]{3,1,2,0:T(8,128)(2,1)}), bf16[64,8,8,256]{3,1,2,0:T(8,128)(2,1)S(1)}, u32[]{:S(2)}, u32[]{:S(2)}) async-start(bf16[64,8,8,256]{3,1,2,0:T(8,128)(2,1)} %constant_dynamic-update-slice_fusion), calls=%async_computation.2 | async-start | bytes 4194304 | tf_op jit(solution)/shard_map/all_to_all | solution.py:63
  201.2 1.6 copy-start.1
